TPU v7x, 128 devices: a whole 4x4x4 slice. The times are simulated.
128 devices in a mesh: grid: 32 (over y, x, core), layer: 4 (over z).
Axes of the slice: x: 4, y: 4, z: 4, core: 2. Of those that a mesh axis runs over, the one named last changes fastest.
Arguments:
- h_blocks: bfloat16 [1024, 8, 128, 128], P('grid', 'layer'), may hold values from -0.09375 to 0.09375
- block_cols: int32 [1024, 8], P('grid', 'layer'), may hold values from 0 to 1023, as said below
- t_now: bfloat16 [131072, 1536], P(('grid', 'layer')), may hold values from -6 to 6
- t_prev: bfloat16 [131072, 1536], P(('grid', 'layer')), may hold values from -6 to 6
Outputs:
- next_term: bfloat16 [131072, 1536], P(('grid', 'layer'))
- after_term: bfloat16 [131072, 1536], P(('grid', 'layer'))
Inputs may be any that keep to these rules, and one draw needn't show every extreme that they name: block_cols[i, 0] = i. With g = i // 32, every block column lies among the block rows g * 32 - 2 to g * 32 + 33 counted cyclically modulo 1024, and both ends of that range are named in every block row.
All inputs are finite; a program needn't handle non-finite values.
Results may differ from a plain program's by a relative error of at most 0.019.
Values may be sent and summed in bfloat16 or wider, within the bound.
No kernel may reach another device: no remote copies, remote signals or barrier semaphores. Data moves between devices by JAX's collectives and lax.ppermute only.
A program may use at most 192 MiB of HBM per device.

v0:
```python
import jax
import jax.numpy as jnp
from jax import lax
from jax.sharding import PartitionSpec as P

KB = 8
HB = 2
NCH = 4


def padded(array, width):
    size, length = (lax.axis_size("grid"), array.shape[0])
    up = [(i, (i + 1) % size) for i in range(size)]
    down = [(j, i) for i, j in up]
    before = lax.ppermute(array[length - width :], "grid", up)
    after = lax.ppermute(array[:width], "grid", down)
    return jnp.concatenate([before, array, after], axis=0)


def own_rows(h_own, rel_own, chunk):
    block_size = h_own.shape[2]
    panel = lax.all_gather(chunk, "layer", axis=0, tiled=True)
    wide = padded(panel, HB * block_size)
    blocks = wide.reshape(wide.shape[0] // block_size, block_size, chunk.shape[1])
    picked = blocks[rel_own]
    acc = jnp.einsum("rsij,rsjc->ric", h_own, picked, preferred_element_type=jnp.float32)
    return acc.reshape(chunk.shape[0], chunk.shape[1])


def shards(h_blocks, block_cols, t_now, t_prev):
    group_rows = h_blocks.shape[0]
    total_blocks = group_rows * lax.axis_size("grid")
    first_block = lax.axis_index("grid") * group_rows
    relative = (block_cols - first_block + HB + total_blocks) % total_blocks
    h_own = lax.all_to_all(h_blocks, "layer", 0, 1, tiled=True)
    rel_own = lax.all_to_all(relative, "layer", 0, 1, tiled=True)
    width = t_now.shape[1]
    step = width // NCH

    def recur(current, previous):
        outs = []
        for c in range(NCH):
            acc = own_rows(h_own, rel_own, current[c])
            outs.append((2.0 * acc - previous[c].astype(jnp.float32)).astype(jnp.bfloat16))
        return outs

    now_chunks = [t_now[:, c * step : (c + 1) * step] for c in range(NCH)]
    prev_chunks = [t_prev[:, c * step : (c + 1) * step] for c in range(NCH)]
    next_chunks = recur(now_chunks, prev_chunks)
    after_chunks = recur(next_chunks, now_chunks)
    return (jnp.concatenate(next_chunks, axis=1), jnp.concatenate(after_chunks, axis=1))


def solution(mesh):
    in_specs = (
        P("grid", "layer", None, None),
        P("grid", "layer"),
        P(("grid", "layer"), None),
        P(("grid", "layer"), None),
    )
    out_specs = (P(("grid", "layer"), None), P(("grid", "layer"), None))
    return jax.shard_map(shards, mesh=mesh, in_specs=in_specs, out_specs=out_specs, check_vma=False)
```

profile of v0, /device:TPU:0, one launch (start us, length us, event | category | flops | bytes accessed | tf_op | source)
XLA Modules:
  0.0 535.9 jit_solution(12677658248927611347)
XLA Ops:
  7.2 3.6 fusion.14
  10.9 0.7 all-gather.13.cloned.1.call-update
  11.7 0.7 all-gather.11.cloned.1.call-update
  12.4 0.5 all-gather.9.cloned.1.call-update
  13.1 10.5 %all_to_all.37 = s32[4,8,2]{1,2,0:T(2,128)S(1)} all-to-all(s32[4,8,2]{1,2,0:T(2,128)S(1)} %copy.9), channel_id=1, replica_groups=mesh['grid'=32,'layer'=4] {'layer'}, dimensions={0} | all-to-all | bytes 512 | tf_op jit(solution)/shard_map/all_to_all | solution.py:36
  23.6 3.6 all-to-all-start.1
  27.4 48.1 %all-to-all-done.1 = bf16[32,2,128,128]{3,2,1,0:T(8,128)(2,1)S(1)} async-done(((bf16[32,2,128,128]{3,2,1,0:T(8,128)(2,1)}), bf16[32,2,128,128]{3,2,1,0:T(8,128)(2,1)S(1)}, u32[]{:S(2)}, u32[]{:S(2)}) %all-to-all-start.1) | async-done | bytes 2097184 | tf_op jit(solution)/shard_map/all_to_all | solution.py:35
  75.5 1.3 copy-done.2
  76.9 1.7 copy.11
  78.6 1.1 fusion.17
  79.8 5.1 collective-permute-start.7
  84.8 32.1 %all-gather.13.cloned.1.call-done = bf16[4096,384]{1,0:T(8,128)(2,1)} async-done(((bf16[1024,384]{1,0:T(8,128)(2,1)}), bf16[4096,384]{1,0:T(8,128)(2,1)}) %all-gather.13.cloned.1.call-update) | async-done | bytes 3145744 | tf_op jit(solution)/shard_map/all_gather | solution.py:22
  117.0 1.8 fusion.16
  118.8 5.1 collective-permute-start.5
  123.8 34.6 %all-gather.11.cloned.1.call-done = bf16[4096,384]{1,0:T(8,128)(2,1)} async-done(((bf16[1024,384]{1,0:T(8,128)(2,1)}), bf16[4096,384]{1,0:T(8,128)(2,1)}) %all-gather.11.cloned.1.call-update) | async-done | bytes 3145744 | tf_op jit(solution)/shard_map/all_gather | solution.py:22
  158.4 1.8 fusion.15
  160.2 40.0 %all-gather.9.cloned.1.call-done = bf16[4096,384]{1,0:T(8,128)(2,1)} async-done(((bf16[1024,384]{1,0:T(8,128)(2,1)}), bf16[4096,384]{1,0:T(8,128)(2,1)}) %all-gather.9.cloned.1.call-update) | async-done | bytes 3145744 | tf_op jit(solution)/shard_map/all_gather | solution.py:22
  200.2 1.8 fusion.13
  202.1 4.1 collective-permute-start.3
  206.2 7.1 %pad_maximum_fusion.3 = bf16[4608,384]{1,0:T(8,128)(2,1)} fusion(bf16[256,384]{1,0:T(8,128)(2,1)S(1)} %collective-permute-done.7, bf16[4096,384]{1,0:T(8,128)(2,1)} %all-gather.15.cloned.1.call-done, bf16[256,384]{1,0:T(8,128)(2,1)S(1)} %collective-permute-done.6), kind=kLoop, calls=%fused_computation.11 | loop fusion | flops 10616832 | bytes 7077888 | tf_op jit(solution)/shard_map/concatenate | solution.py:17
  213.3 6.1 %gather_fusion.3 = bf16[64,128,384]{2,1,0:T(8,128)(2,1)} fusion(bf16[36,128,384]{2,1,0:T(8,128)(2,1)} %bitcast.132, s32[1024]{0:T(1024)S(1)} %pad_clamp_fusion), kind=kCustom, calls=%fused_computation.3 | custom fusion | bytes 12583168 | tf_op jit(solution)/shard_map/gather | solution.py:25
  219.4 5.6 %collective-permute-start.1 = (bf16[256,384]{1,0:T(8,128)(2,1)S(1)}, bf16[256,384]{1,0:T(8,128)(2,1)S(1)}, u32[]{:S(2)}, u32[]{:S(2)}) collective-permute-start(bf16[256,384]{1,0:T(8,128)(2,1)S(1)} %copy-done.16), channel_id=1, source_target_pairs={{4,0},{8,4},{12,8},{16,12},{20,16},{24,20},{28,24},{32,28},{36,32}... | collective-permute-start | bytes 589832 | tf_op jit(solution)/shard_map/ppermute | solution.py:16
  224.9 7.0 %pad_maximum_fusion.2 = bf16[4608,384]{1,0:T(8,128)(2,1)} fusion(bf16[256,384]{1,0:T(8,128)(2,1)S(1)} %collective-permute-done.5, bf16[4096,384]{1,0:T(8,128)(2,1)} %all-gather.13.cloned.1.call-done, bf16[256,384]{1,0:T(8,128)(2,1)S(1)} %collective-permute-done.4), kind=kLoop, calls=%fused_computation.10 | loop fusion | flops 10616832 | bytes 7077888 | tf_op jit(solution)/shard_map/concatenate | solution.py:17
  232.0 6.1 %gather_fusion.2 = bf16[64,128,384]{2,1,0:T(8,128)(2,1)} fusion(bf16[36,128,384]{2,1,0:T(8,128)(2,1)} %bitcast.133, s32[1024]{0:T(1024)S(1)} %pad_clamp_fusion), kind=kCustom, calls=%fused_computation.2 | custom fusion | bytes 12583168 | tf_op jit(solution)/shard_map/gather | solution.py:25
  238.1 5.3 bitcast_multiply_fusion.4
  243.4 2.5 bitcast_multiply_fusion.5
  245.9 6.3 %pad_maximum_fusion.1 = bf16[4608,384]{1,0:T(8,128)(2,1)} fusion(bf16[256,384]{1,0:T(8,128)(2,1)S(1)} %collective-permute-done.3, bf16[4096,384]{1,0:T(8,128)(2,1)S(1)} %copy-done.11, bf16[256,384]{1,0:T(8,128)(2,1)S(1)} %collective-permute-done.2), kind=kLoop, calls=%fused_computation.9 | loop fusion | flops 10616832 | bytes 7077888 | tf_op jit(solution)/shard_map/concatenate | solution.py:17
  252.2 6.1 %gather_fusion.1 = bf16[64,128,384]{2,1,0:T(8,128)(2,1)} fusion(bf16[36,128,384]{2,1,0:T(8,128)(2,1)} %bitcast.134, s32[1024]{0:T(1024)S(1)} %pad_clamp_fusion), kind=kCustom, calls=%fused_computation.1 | custom fusion | bytes 12583168 | tf_op jit(solution)/shard_map/gather | solution.py:25
  258.3 5.3 bitcast_multiply_fusion.6
  263.6 6.5 %pad_maximum_fusion = bf16[4608,384]{1,0:T(8,128)(2,1)} fusion(bf16[256,384]{1,0:T(8,128)(2,1)S(1)} %collective-permute-done.1, bf16[4096,384]{1,0:T(8,128)(2,1)S(1)} %copy-done.10, bf16[256,384]{1,0:T(8,128)(2,1)S(1)} %collective-permute-done), kind=kLoop, calls=%fused_computation.8 | loop fusion | flops 10616832 | bytes 7077888 | tf_op jit(solution)/shard_map/concatenate | solution.py:17
  270.1 6.1 %gather_fusion = bf16[64,128,384]{2,1,0:T(8,128)(2,1)} fusion(bf16[36,128,384]{2,1,0:T(8,128)(2,1)} %bitcast.135, s32[1024]{0:T(1024)S(1)} %pad_clamp_fusion), kind=kCustom, calls=%fused_computation | custom fusion | bytes 12583168 | tf_op jit(solution)/shard_map/gather | solution.py:25
  276.2 4.2 bitcast_multiply_fusion.7
  280.4 0.9 copy-done.15
  281.3 2.2 fusion.7
  283.5 0.5 all-gather.21.cloned.1.call-update
  284.1 0.7 all-gather.19.cloned.1.call-update
  284.9 0.7 all-gather.17.cloned.1.call-update
  285.6 3.0 pad_maximum_fusion.8
  288.6 29.9 %all-gather.23.cloned.1.call-done = bf16[4096,384]{1,0:T(8,128)(2,1)} async-done(((bf16[1024,384]{1,0:T(8,128)(2,1)}), bf16[4096,384]{1,0:T(8,128)(2,1)}) %all-gather.23.cloned.1.call-update) | async-done | bytes 3145744 | tf_op jit(solution)/shard_map/all_gather | solution.py:22
  318.5 1.1 fusion.12
  319.7 5.1 collective-permute-start.15
  324.7 35.1 %all-gather.21.cloned.1.call-done = bf16[4096,384]{1,0:T(8,128)(2,1)} async-done(((bf16[1024,384]{1,0:T(8,128)(2,1)}), bf16[4096,384]{1,0:T(8,128)(2,1)}) %all-gather.21.cloned.1.call-update) | async-done | bytes 3145744 | tf_op jit(solution)/shard_map/all_gather | solution.py:22
  359.8 1.8 fusion.11
  361.6 5.1 collective-permute-start.13
  366.7 34.6 %all-gather.19.cloned.1.call-done = bf16[4096,384]{1,0:T(8,128)(2,1)} async-done(((bf16[1024,384]{1,0:T(8,128)(2,1)}), bf16[4096,384]{1,0:T(8,128)(2,1)}) %all-gather.19.cloned.1.call-update) | async-done | bytes 3145744 | tf_op jit(solution)/shard_map/all_gather | solution.py:22
  401.2 1.8 fusion.10
  403.1 40.2 %all-gather.17.cloned.1.call-done = bf16[4096,384]{1,0:T(8,128)(2,1)} async-done(((bf16[1024,384]{1,0:T(8,128)(2,1)}), bf16[4096,384]{1,0:T(8,128)(2,1)}) %all-gather.17.cloned.1.call-update) | async-done | bytes 3145744 | tf_op jit(solution)/shard_map/all_gather | solution.py:22
  443.2 1.8 fusion.9
  445.0 4.1 collective-permute-start.11
  449.2 7.1 %pad_maximum_fusion.7 = bf16[4608,384]{1,0:T(8,128)(2,1)} fusion(bf16[256,384]{1,0:T(8,128)(2,1)S(1)} %collective-permute-done.15, bf16[4096,384]{1,0:T(8,128)(2,1)} %all-gather.23.cloned.1.call-done, bf16[256,384]{1,0:T(8,128)(2,1)S(1)} %collective-permute-done.14), kind=kLoop, calls=%fused_computation.15 | loop fusion | flops 10616832 | bytes 7077888 | tf_op jit(solution)/shard_map/concatenate | solution.py:17
  456.3 6.1 %gather_fusion.7 = bf16[64,128,384]{2,1,0:T(8,128)(2,1)} fusion(bf16[36,128,384]{2,1,0:T(8,128)(2,1)} %bitcast.136, s32[1024]{0:T(1024)S(1)} %pad_clamp_fusion), kind=kCustom, calls=%fused_computation.7 | custom fusion | bytes 12583168 | tf_op jit(solution)/shard_map/gather | solution.py:25
  462.3 5.4 %bitcast_multiply_fusion = f32[8,384,128]{1,2,0:T(8,128)} fusion(bf16[8,8,128,128]{3,2,1,0:T(8,128)(2,1)S(1)} %bitcast.119, bf16[8,8,128,384]{3,2,1,0:T(8,128)(2,1)} %bitcast.128), kind=kOutput, calls=%fused_computation.34 | convolution fusion | flops 805699584 | bytes 9961472 | tf_op jit(solution)/shard_map/rsij,rsjc->ric/dot_general | solution.py:26
  467.7 5.1 collective-permute-start.9
  472.8 6.5 %pad_maximum_fusion.6 = bf16[4608,384]{1,0:T(8,128)(2,1)} fusion(bf16[256,384]{1,0:T(8,128)(2,1)S(1)} %collective-permute-done.13, bf16[4096,384]{1,0:T(8,128)(2,1)S(1)} %copy-done.14, bf16[256,384]{1,0:T(8,128)(2,1)S(1)} %collective-permute-done.12), kind=kLoop, calls=%fused_computation.14 | loop fusion | flops 10616832 | bytes 7077888 | tf_op jit(solution)/shard_map/concatenate | solution.py:17
  479.2 6.1 %gather_fusion.6 = bf16[64,128,384]{2,1,0:T(8,128)(2,1)} fusion(bf16[36,128,384]{2,1,0:T(8,128)(2,1)} %bitcast.137, s32[1024]{0:T(1024)S(1)} %pad_clamp_fusion), kind=kCustom, calls=%fused_computation.6 | custom fusion | bytes 12583168 | tf_op jit(solution)/shard_map/gather | solution.py:25
  485.3 5.4 %bitcast_multiply_fusion.1 = f32[8,384,128]{1,2,0:T(8,128)} fusion(bf16[8,8,128,128]{3,2,1,0:T(8,128)(2,1)S(1)} %bitcast.120, bf16[8,8,128,384]{3,2,1,0:T(8,128)(2,1)} %bitcast.129), kind=kOutput, calls=%fused_computation.35 | convolution fusion | flops 805699584 | bytes 9961472 | tf_op jit(solution)/shard_map/rsij,rsjc->ric/dot_general | solution.py:26
  490.7 6.3 %pad_maximum_fusion.5 = bf16[4608,384]{1,0:T(8,128)(2,1)} fusion(bf16[256,384]{1,0:T(8,128)(2,1)S(1)} %collective-permute-done.11, bf16[4096,384]{1,0:T(8,128)(2,1)S(1)} %copy-done.13, bf16[256,384]{1,0:T(8,128)(2,1)S(1)} %collective-permute-done.10), kind=kLoop, calls=%fused_computation.13 | loop fusion | flops 10616832 | bytes 7077888 | tf_op jit(solution)/shard_map/concatenate | solution.py:17
  497.0 6.1 %gather_fusion.5 = bf16[64,128,384]{2,1,0:T(8,128)(2,1)} fusion(bf16[36,128,384]{2,1,0:T(8,128)(2,1)} %bitcast.138, s32[1024]{0:T(1024)S(1)} %pad_clamp_fusion), kind=kCustom, calls=%fused_computation.5 | custom fusion | bytes 12583168 | tf_op jit(solution)/shard_map/gather | solution.py:25
  503.0 5.3 bitcast_multiply_fusion.2
  508.4 6.5 %pad_maximum_fusion.4 = bf16[4608,384]{1,0:T(8,128)(2,1)} fusion(bf16[256,384]{1,0:T(8,128)(2,1)S(1)} %collective-permute-done.9, bf16[4096,384]{1,0:T(8,128)(2,1)S(1)} %copy-done.12, bf16[256,384]{1,0:T(8,128)(2,1)S(1)} %collective-permute-done.8), kind=kLoop, calls=%fused_computation.12 | loop fusion | flops 10616832 | bytes 7077888 | tf_op jit(solution)/shard_map/concatenate | solution.py:17
  514.9 6.1 %gather_fusion.4 = bf16[64,128,384]{2,1,0:T(8,128)(2,1)} fusion(bf16[36,128,384]{2,1,0:T(8,128)(2,1)} %bitcast.131, s32[1024]{0:T(1024)S(1)} %pad_clamp_fusion), kind=kCustom, calls=%fused_computation.4 | custom fusion | bytes 12583168 | tf_op jit(solution)/shard_map/gather | solution.py:25
  521.0 4.2 bitcast_multiply_fusion.3
  526.1 0.7 fusion.3
  526.8 1.8 pad_maximum_fusion.9
  (78 shorter events, 1.8 us)
Async XLA Ops:
  7.2 5.8 %copy-start.18 = (s32[32,2]{0,1:T(2,128)S(1)}, s32[32,2]{0,1:T(2,128)}, u32[]{:S(2)}) copy-start(s32[32,2]{0,1:T(2,128)} %param.5) | copy-start | bytes 772
  7.2 71.4 %all-gather.15.cloned.1.call-start = ((), (), s32[]{:S(2)}) async-start(), calls=%async_computation.5 | async-start | bytes 3932160 | tf_op jit(solution)/shard_map/all_gather | solution.py:22
  10.9 106.1 %all-gather.13.cloned.1.call-start = ((), (), s32[]{:S(2)}) async-start(), calls=%async_computation.4 | async-start | bytes 3932160 | tf_op jit(solution)/shard_map/all_gather | solution.py:22
  11.6 146.8 %all-gather.11.cloned.1.call-start = ((), (), s32[]{:S(2)}) async-start(), calls=%async_computation.3 | async-start | bytes 3932160 | tf_op jit(solution)/shard_map/all_gather | solution.py:22
  12.4 187.9 %all-gather.9.cloned.1.call-start = ((), (), s32[]{:S(2)}) async-start(), calls=%async_computation.2 | async-start | bytes 3932160 | tf_op jit(solution)/shard_map/all_gather | solution.py:22
  23.6 52.0 %all-to-all-start.1 = ((bf16[32,2,128,128]{3,2,1,0:T(8,128)(2,1)}), bf16[32,2,128,128]{3,2,1,0:T(8,128)(2,1)S(1)}, u32[]{:S(2)}, u32[]{:S(2)}) async-start(bf16[32,2,128,128]{3,2,1,0:T(8,128)(2,1)} %param.4), calls=%async_computation.1 | async-start | bytes 4194304 | tf_op jit(solution)/shard_map/all_to_all | solution.py:35
  27.2 291.3 %all-gather.23.cloned.1.call-start = ((), (), s32[]{:S(2)}) async-start(), calls=%async_computation.9 | async-start | bytes 3932160 | tf_op jit(solution)/shard_map/all_gather | solution.py:22
  75.5 1.3 copy-start.2
  79.7 122.4 %collective-permute-start.6 = (bf16[256,384]{1,0:T(8,128)(2,1)S(1)}, bf16[256,384]{1,0:T(8,128)(2,1)S(1)}, u32[]{:S(2)}, u32[]{:S(2)}) collective-permute-start(bf16[256,384]{1,0:T(8,128)(2,1)S(1)} %get-tuple-element.28), channel_id=1, source_target_pairs={{0,4},{4,8},{8,12},{12,16},{16,20},{20,24},{24,28},{28,32},{32,36}... | collective-permute-start | bytes 589832 | tf_op jit(solution)/shard_map/ppermute | solution.py:15
  79.8 126.4 %collective-permute-start.7 = (bf16[256,384]{1,0:T(8,128)(2,1)S(1)}, bf16[256,384]{1,0:T(8,128)(2,1)S(1)}, u32[]{:S(2)}, u32[]{:S(2)}) collective-permute-start(bf16[256,384]{1,0:T(8,128)(2,1)S(1)} %get-tuple-element.29), channel_id=1, source_target_pairs={{4,0},{8,4},{12,8},{16,12},{20,16},{24,20},{28,24},{32,28},{36,32}... | collective-permute-start | bytes 589832 | tf_op jit(solution)/shard_map/ppermute | solution.py:16
  118.8 100.6 %collective-permute-start.4 = (bf16[256,384]{1,0:T(8,128)(2,1)}, bf16[256,384]{1,0:T(8,128)(2,1)S(1)}, u32[]{:S(2)}, u32[]{:S(2)}) collective-permute-start(bf16[256,384]{1,0:T(8,128)(2,1)} %get-tuple-element.26), channel_id=1, source_target_pairs={{0,4},{4,8},{8,12},{12,16},{16,20},{20,24},{24,28},{28,32},{32,36}... | collective-permute-start | bytes 589832 | tf_op jit(solution)/shard_map/ppermute | solution.py:15
  118.8 106.2 %collective-permute-start.5 = (bf16[256,384]{1,0:T(8,128)(2,1)}, bf16[256,384]{1,0:T(8,128)(2,1)S(1)}, u32[]{:S(2)}, u32[]{:S(2)}) collective-permute-start(bf16[256,384]{1,0:T(8,128)(2,1)} %get-tuple-element.27), channel_id=1, source_target_pairs={{4,0},{8,4},{12,8},{16,12},{20,16},{24,20},{28,24},{32,28},{36,32}... | collective-permute-start | bytes 589832 | tf_op jit(solution)/shard_map/ppermute | solution.py:16
  160.2 85.7 %collective-permute-start.2 = (bf16[256,384]{1,0:T(8,128)(2,1)}, bf16[256,384]{1,0:T(8,128)(2,1)S(1)}, u32[]{:S(2)}, u32[]{:S(2)}) collective-permute-start(bf16[256,384]{1,0:T(8,128)(2,1)} %get-tuple-element.24), channel_id=1, source_target_pairs={{0,4},{4,8},{8,12},{12,16},{16,20},{20,24},{24,28},{28,32},{32,36}... | collective-permute-start | bytes 589832 | tf_op jit(solution)/shard_map/ppermute | solution.py:15
  202.1 43.9 %collective-permute-start.3 = (bf16[256,384]{1,0:T(8,128)(2,1)}, bf16[256,384]{1,0:T(8,128)(2,1)S(1)}, u32[]{:S(2)}, u32[]{:S(2)}) collective-permute-start(bf16[256,384]{1,0:T(8,128)(2,1)} %get-tuple-element.25), channel_id=1, source_target_pairs={{4,0},{8,4},{12,8},{16,12},{20,16},{24,20},{28,24},{32,28},{36,32}... | collective-permute-start | bytes 589832 | tf_op jit(solution)/shard_map/ppermute | solution.py:16
  206.2 57.4 %collective-permute-start = (bf16[256,384]{1,0:T(8,128)(2,1)}, bf16[256,384]{1,0:T(8,128)(2,1)S(1)}, u32[]{:S(2)}, u32[]{:S(2)}) collective-permute-start(bf16[256,384]{1,0:T(8,128)(2,1)} %get-tuple-element.18), channel_id=1, source_target_pairs={{0,4},{4,8},{8,12},{12,16},{16,20},{20,24},{24,28},{28,32},{32,36}... | collective-permute-start | bytes 589832 | tf_op jit(solution)/shard_map/ppermute | solution.py:15
  213.3 6.1 %copy-start.16 = (bf16[256,384]{1,0:T(8,128)(2,1)S(1)}, bf16[256,384]{1,0:T(8,128)(2,1)}, u32[]{:S(2)}) copy-start(bf16[256,384]{1,0:T(8,128)(2,1)} %get-tuple-element.19) | copy-start | bytes 589828
  219.4 44.2 %collective-permute-start.1 = (bf16[256,384]{1,0:T(8,128)(2,1)S(1)}, bf16[256,384]{1,0:T(8,128)(2,1)S(1)}, u32[]{:S(2)}, u32[]{:S(2)}) collective-permute-start(bf16[256,384]{1,0:T(8,128)(2,1)S(1)} %copy-done.16), channel_id=1, source_target_pairs={{4,0},{8,4},{12,8},{16,12},{20,16},{24,20},{28,24},{32,28},{36,32}... | collective-permute-start | bytes 589832 | tf_op jit(solution)/shard_map/ppermute | solution.py:16
  238.1 5.3 copy-start
  243.4 2.5 copy-start.11
  258.3 5.4 copy-start.10
  276.1 4.2 copy-start.5
  276.1 4.2 copy-start.6
  276.2 4.2 copy-start.8
  276.2 5.1 copy-start.15
  283.5 2.1 copy-start.9
  283.5 76.3 %all-gather.21.cloned.1.call-start = ((), (), s32[]{:S(2)}) async-start(), calls=%async_computation.8 | async-start | bytes 3932160 | tf_op jit(solution)/shard_map/all_gather | solution.py:22
  284.1 117.2 %all-gather.19.cloned.1.call-start = ((), (), s32[]{:S(2)}) async-start(), calls=%async_computation.7 | async-start | bytes 3932160 | tf_op jit(solution)/shard_map/all_gather | solution.py:22
  284.8 158.4 %all-gather.17.cloned.1.call-start = ((), (), s32[]{:S(2)}) async-start(), calls=%async_computation.6 | async-start | bytes 3932160 | tf_op jit(solution)/shard_map/all_gather | solution.py:22
  319.6 125.5 %collective-permute-start.14 = (bf16[256,384]{1,0:T(8,128)(2,1)S(1)}, bf16[256,384]{1,0:T(8,128)(2,1)S(1)}, u32[]{:S(2)}, u32[]{:S(2)}) collective-permute-start(bf16[256,384]{1,0:T(8,128)(2,1)S(1)} %get-tuple-element.12), channel_id=1, source_target_pairs={{0,4},{4,8},{8,12},{12,16},{16,20},{20,24},{24,28},{28,32},{32,36}... | collective-permute-start | bytes 589832 | tf_op jit(solution)/shard_map/ppermute | solution.py:15
  319.7 129.5 %collective-permute-start.15 = (bf16[256,384]{1,0:T(8,128)(2,1)S(1)}, bf16[256,384]{1,0:T(8,128)(2,1)S(1)}, u32[]{:S(2)}, u32[]{:S(2)}) collective-permute-start(bf16[256,384]{1,0:T(8,128)(2,1)S(1)} %get-tuple-element.13), channel_id=1, source_target_pairs={{4,0},{8,4},{12,8},{16,12},{20,16},{24,20},{28,24},{32,28},{36,32}... | collective-permute-start | bytes 589832 | tf_op jit(solution)/shard_map/ppermute | solution.py:16
  361.6 106.1 %collective-permute-start.12 = (bf16[256,384]{1,0:T(8,128)(2,1)}, bf16[256,384]{1,0:T(8,128)(2,1)S(1)}, u32[]{:S(2)}, u32[]{:S(2)}) collective-permute-start(bf16[256,384]{1,0:T(8,128)(2,1)} %get-tuple-element.10), channel_id=1, source_target_pairs={{0,4},{4,8},{8,12},{12,16},{16,20},{20,24},{24,28},{28,32},{32,36}... | collective-permute-start | bytes 589832 | tf_op jit(solution)/shard_map/ppermute | solution.py:15
  361.6 111.1 %collective-permute-start.13 = (bf16[256,384]{1,0:T(8,128)(2,1)}, bf16[256,384]{1,0:T(8,128)(2,1)S(1)}, u32[]{:S(2)}, u32[]{:S(2)}) collective-permute-start(bf16[256,384]{1,0:T(8,128)(2,1)} %get-tuple-element.11), channel_id=1, source_target_pairs={{4,0},{8,4},{12,8},{16,12},{20,16},{24,20},{28,24},{32,28},{36,32}... | collective-permute-start | bytes 589832 | tf_op jit(solution)/shard_map/ppermute | solution.py:16
  403.1 87.6 %collective-permute-start.10 = (bf16[256,384]{1,0:T(8,128)(2,1)}, bf16[256,384]{1,0:T(8,128)(2,1)S(1)}, u32[]{:S(2)}, u32[]{:S(2)}) collective-permute-start(bf16[256,384]{1,0:T(8,128)(2,1)} %get-tuple-element.8), channel_id=1, source_target_pairs={{0,4},{4,8},{8,12},{12,16},{16,20},{20,24},{24,28},{28,32},{32,36}... | collective-permute-start | bytes 589832 | tf_op jit(solution)/shard_map/ppermute | solution.py:15
  445.0 45.6 %collective-permute-start.11 = (bf16[256,384]{1,0:T(8,128)(2,1)}, bf16[256,384]{1,0:T(8,128)(2,1)S(1)}, u32[]{:S(2)}, u32[]{:S(2)}) collective-permute-start(bf16[256,384]{1,0:T(8,128)(2,1)} %get-tuple-element.9), channel_id=1, source_target_pairs={{4,0},{8,4},{12,8},{16,12},{20,16},{24,20},{28,24},{32,28},{36,32}... | collective-permute-start | bytes 589832 | tf_op jit(solution)/shard_map/ppermute | solution.py:16
  449.2 59.2 %collective-permute-start.8 = (bf16[256,384]{1,0:T(8,128)(2,1)}, bf16[256,384]{1,0:T(8,128)(2,1)S(1)}, u32[]{:S(2)}, u32[]{:S(2)}) collective-permute-start(bf16[256,384]{1,0:T(8,128)(2,1)} %get-tuple-element.6), channel_id=1, source_target_pairs={{0,4},{4,8},{8,12},{12,16},{16,20},{20,24},{24,28},{28,32},{32,36}... | collective-permute-start | bytes 589832 | tf_op jit(solution)/shard_map/ppermute | solution.py:15
  462.3 5.4 %copy-start.17 = (bf16[256,384]{1,0:T(8,128)(2,1)S(1)}, bf16[256,384]{1,0:T(8,128)(2,1)}, u32[]{:S(2)}) copy-start(bf16[256,384]{1,0:T(8,128)(2,1)} %get-tuple-element.7) | copy-start | bytes 589828
  462.3 10.4 %copy-start.14 = (bf16[4096,384]{1,0:T(8,128)(2,1)S(1)}, bf16[4096,384]{1,0:T(8,128)(2,1)}, u32[]{:S(2)}) copy-start(bf16[4096,384]{1,0:T(8,128)(2,1)} %all-gather.21.cloned.1.call-done) | copy-start | bytes 9437188
  467.7 40.7 %collective-permute-start.9 = (bf16[256,384]{1,0:T(8,128)(2,1)S(1)}, bf16[256,384]{1,0:T(8,128)(2,1)S(1)}, u32[]{:S(2)}, u32[]{:S(2)}) collective-permute-start(bf16[256,384]{1,0:T(8,128)(2,1)S(1)} %copy-done.17), channel_id=1, source_target_pairs={{4,0},{8,4},{12,8},{16,12},{20,16},{24,20},{28,24},{32,28},{36,32}... | collective-permute-start | bytes 589832 | tf_op jit(solution)/shard_map/ppermute | solution.py:16
  485.3 5.4 %copy-start.13 = (bf16[4096,384]{1,0:T(8,128)(2,1)S(1)}, bf16[4096,384]{1,0:T(8,128)(2,1)}, u32[]{:S(2)}) copy-start(bf16[4096,384]{1,0:T(8,128)(2,1)} %all-gather.19.cloned.1.call-done) | copy-start | bytes 9437188
  503.0 5.4 copy-start.12
  521.0 4.2 copy-start.1
  521.0 4.2 copy-start.3
  521.0 4.6 copy-start.4
  521.0 5.1 copy-start.7
Sparse Core Ops, SparseCore 0:
  11.0 64.1 all-gather.14
  76.8 40.1 all-gather.12
  118.6 39.7 all-gather.10
  160.5 39.7 all-gather.8
  283.6 34.8 all-gather.22
  320.0 39.7 all-gather.20
  361.5 39.7 all-gather.18
  403.5 39.7 all-gather.16
where the time goes:
time: 542 us; the launch traced here: 536 us
  waiting for transfers between devices  298 us (55%)
  local copies, waits for them, and re-layouts  70.3 us (13%)
  other arithmetic  61 us (11%)
  starting transfers between devices  43.2 us (8%)
  matrix products  37.6 us (7%)
  between operations  14.8 us (3%)
  blocking collectives  10.5 us (2%)
    all_gather x8, waiting for transfers between devices, own_rows(): panel = lax.all_gather(chunk, 'layer', axis=0, tiled=True)  246 us
    concatenate x8, other arithmetic, padded(): return jnp.concatenate([before, array, after], axis=0)  53.2 us
    gather x8, local copies, waits for them, and re-layouts, own_rows(): picked = blocks[rel_own]  48.5 us
    all_to_all x1, waiting for transfers between devices, shards(): h_own = lax.all_to_all(h_blocks, 'layer', 0, 1, tiled=True)  48.1 us
    ppermute x8, starting transfers between devices, padded(): after = lax.ppermute(array[:width], 'grid', down)  39.1 us
    dot_general x8, matrix products, own_rows(): jnp.einsum('rsij,rsjc->ric', h_own, picked, preferred_element_type=jnp.fl...  37.6 us
    slice x8, local copies, waits for them, and re-layouts, padded(): before = lax.ppermute(array[length - width:], 'grid', up)  13 us
  transfers between devices with their start and end apart: 25, of which 8 were waited for; matrix products, arithmetic and copies ran while one was open for 23% of the time, Pallas kernels for 0%

commit v1 on v0

--- a/solution.py
+++ b/solution.py
@@ -6,6 +6,28 @@
 KB = 8
 HB = 2
 NCH = 4
+
+
+def laid_out(tiles, dim):
+    dims = list(tiles.shape[1:])
+    dims[dim] *= tiles.shape[0]
+    return jnp.moveaxis(tiles, 0, dim).reshape(dims)
+
+
+def collect(array, axis, dim):
+    size = lax.axis_size(axis)
+    pairs = [(i, (i + 1) % size) for i in range(size)]
+    back = [(b, a) for a, b in pairs]
+    lower, upper = ([], [])
+    for step in range(size - 1):
+        if step % 2 == 0:
+            lower.append(lax.ppermute(lower[-1] if lower else array, axis, pairs))
+        else:
+            upper.append(lax.ppermute(upper[-1] if upper else array, axis, back))
+    blocks = jnp.stack([*lower[::-1], array, *upper])
+    shift = lax.axis_index(axis) - len(lower)
+    blocks = blocks[(jnp.arange(size) - shift) % size]
+    return laid_out(blocks, dim)
 
 
 def padded(array, width):
@@ -19,7 +41,7 @@
 
 def own_rows(h_own, rel_own, chunk):
     block_size = h_own.shape[2]
-    panel = lax.all_gather(chunk, "layer", axis=0, tiled=True)
+    panel = collect(chunk, "layer", 0)
     wide = padded(panel, HB * block_size)
     blocks = wide.reshape(wide.shape[0] // block_size, block_size, chunk.shape[1])
     picked = blocks[rel_own]

time: 542 us -> 500 us (0.923)
  waiting for transfers between devices: 298 us -> 147 us
  blocking collectives: 10.5 us -> 50.7 us
  local copies, waits for them, and re-layouts: 70.3 us -> 109 us
  starting transfers between devices: 43.2 us -> 68.6 us
  other arithmetic: 61 us -> 77.2 us
  between operations: 14.8 us -> 1.08 us
    all_gather x8 -> x0, waiting for transfers between devices: 246 us -> none  [own_rows(): panel = lax.all_gather(chunk, 'layer', axis=0, tiled=True)]
    ppermute x0 -> x24, waiting for transfers between devices: none -> 147 us  [the longest x16 120 us: collect(): lower.append(lax.ppermute(lower[-1] if lower else array, axis, pairs))]
    all_to_all x1, waiting for transfers between devices: 48.1 us -> 0.01 us  [shards(): h_own = lax.all_to_all(h_blocks, 'layer', 0, 1, tiled=True)]
    all_to_all x1, blocking collectives: 10.5 us -> 50.7 us  [shards(): rel_own = lax.all_to_all(relative, 'layer', 0, 1, tiled=True)]
    gather x0 -> x8, local copies, waits for them, and re-layouts: none -> 36.4 us  [collect(): blocks = blocks[(jnp.arange(size) - shift) % size]]
    another operation x0 -> x8, other arithmetic: none -> 24.9 us  [collect(): blocks = jnp.stack([*lower[::-1], array, *upper])]
    ppermute x0 -> x24, starting transfers between devices: none -> 24.4 us  [the longest x8 18.9 us: collect(): upper.append(lax.ppermute(upper[-1] if upper else array, axis, back))]
    concatenate x8, other arithmetic: 53.2 us -> 44.9 us  [padded(): return jnp.concatenate([before, array, after], axis=0)]
  transfers between devices with their start and end apart: 25 -> 41, of which waited for: 8 -> 10; matrix products, arithmetic and copies ran while one was open for 23% -> 36% of each run, Pallas kernels for 0% -> 0%
where the time goes in v1:
time: 500 us; the launch traced here: 491 us
  waiting for transfers between devices  147 us (29%)
  local copies, waits for them, and re-layouts  109 us (22%)
  other arithmetic  77.2 us (15%)
  starting transfers between devices  68.6 us (14%)
  blocking collectives  50.7 us (10%)
  matrix products  37.7 us (8%)
    ppermute x16, waiting for transfers between devices, collect(): lower.append(lax.ppermute(lower[-1] if lower else array, axis, pairs))  120 us
    all_to_all x1, blocking collectives, shards(): rel_own = lax.all_to_all(relative, 'layer', 0, 1, tiled=True)  50.7 us
    gather x8, local copies, waits for them, and re-layouts, own_rows(): picked = blocks[rel_own]  48.5 us
    concatenate x8, other arithmetic, padded(): return jnp.concatenate([before, array, after], axis=0)  44.9 us
    ppermute x8, starting transfers between devices, padded(): after = lax.ppermute(array[:width], 'grid', down)  40.4 us
    dot_general x8, matrix products, own_rows(): jnp.einsum('rsij,rsjc->ric', h_own, picked, preferred_element_type=jnp.fl...  37.7 us
    gather x8, local copies, waits for them, and re-layouts, collect(): blocks = blocks[(jnp.arange(size) - shift) % size]  36.4 us
    ppermute x8, waiting for transfers between devices, collect(): upper.append(lax.ppermute(upper[-1] if upper else array, axis, back))  26.8 us
  transfers between devices with their start and end apart: 41, of which 10 were waited for; matrix products, arithmetic and copies ran while one was open for 36% of the time, Pallas kernels for 0%

profile of v1, /device:TPU:0, one launch (start us, length us, event | category | flops | bytes accessed | tf_op | source)
XLA Modules:
  0.0 490.8 jit_solution(12283766444547096611)
XLA Ops:
  0.6 4.4 slice_bitcast_fusion.3
  11.1 16.9 %collective-permute-done.10 = bf16[1024,384]{1,0:T(8,128)(2,1)} collective-permute-done((bf16[1024,384]{1,0:T(8,128)(2,1)}, bf16[1024,384]{1,0:T(8,128)(2,1)}, u32[]{:S(2)}, u32[]{:S(2)}) %collective-permute-start.10) | collective-permute-done | bytes 786464 | tf_op jit(solution)/shard_map/ppermute | solution.py:24
  28.1 50.7 %all_to_all.37 = s32[4,8,2]{1,2,0:T(2,128)S(1)} all-to-all(s32[4,8,2]{1,2,0:T(2,128)S(1)} %copy.9), channel_id=1, replica_groups=mesh['grid'=32,'layer'=4] {'layer'}, dimensions={0} | all-to-all | bytes 512 | tf_op jit(solution)/shard_map/all_to_all | solution.py:58
  78.8 3.6 all-to-all-start.1
  82.4 3.2 collective-permute-start.17
  86.7 2.6 collective-permute-start.7
  89.3 3.3 pad_maximum_fusion.10
  92.5 4.5 gather_fusion.4
  98.9 26.7 %collective-permute-done.17 = bf16[1024,384]{1,0:T(8,128)(2,1)} collective-permute-done((bf16[1024,384]{1,0:T(8,128)(2,1)}, bf16[1024,384]{1,0:T(8,128)(2,1)}, u32[]{:S(2)}, u32[]{:S(2)}) %collective-permute-start.17) | collective-permute-done | bytes 786464 | tf_op jit(solution)/shard_map/ppermute | solution.py:26
  127.6 16.0 %collective-permute-done.16 = bf16[1024,384]{1,0:T(8,128)(2,1)} collective-permute-done((bf16[1024,384]{1,0:T(8,128)(2,1)}, bf16[1024,384]{1,0:T(8,128)(2,1)}, u32[]{:S(2)}, u32[]{:S(2)}) %collective-permute-start.16) | collective-permute-done | bytes 786464 | tf_op jit(solution)/shard_map/ppermute | solution.py:24
  143.6 3.3 pad_maximum_fusion.11
  150.0 4.6 gather_fusion.6
  156.4 5.1 %collective-permute-start.14 = (bf16[256,384]{1,0:T(8,128)(2,1)}, bf16[256,384]{1,0:T(8,128)(2,1)}, u32[]{:S(2)}, u32[]{:S(2)}) collective-permute-start(bf16[256,384]{1,0:T(8,128)(2,1)} %get-tuple-element.31), channel_id=1, source_target_pairs={{4,0},{8,4},{12,8},{16,12},{20,16},{24,20},{28,24},{32,28},{36,32}... | collective-permute-start | bytes 589832 | tf_op jit(solution)/shard_map/ppermute | solution.py:38
  161.5 3.3 pad_maximum_fusion.9
  164.8 4.5 gather_fusion.2
  171.1 5.1 %collective-permute-start.19 = (bf16[256,384]{1,0:T(8,128)(2,1)}, bf16[256,384]{1,0:T(8,128)(2,1)}, u32[]{:S(2)}, u32[]{:S(2)}) collective-permute-start(bf16[256,384]{1,0:T(8,128)(2,1)} %get-tuple-element.33), channel_id=1, source_target_pairs={{4,0},{8,4},{12,8},{16,12},{20,16},{24,20},{28,24},{32,28},{36,32}... | collective-permute-start | bytes 589832 | tf_op jit(solution)/shard_map/ppermute | solution.py:38
  176.2 3.1 pad_maximum_fusion.8
  179.3 4.6 gather_fusion
  185.6 5.1 %collective-permute-start.9 = (bf16[256,384]{1,0:T(8,128)(2,1)S(1)}, bf16[256,384]{1,0:T(8,128)(2,1)S(1)}, u32[]{:S(2)}, u32[]{:S(2)}) collective-permute-start(bf16[256,384]{1,0:T(8,128)(2,1)S(1)} %copy-done.15), channel_id=1, source_target_pairs={{4,0},{8,4},{12,8},{16,12},{20,16},{24,20},{28,24},{32,28},{36,32}... | collective-permute-start | bytes 589832 | tf_op jit(solution)/shard_map/ppermute | solution.py:38
  190.9 5.0 %pad_maximum_fusion.2 = bf16[4608,384]{1,0:T(8,128)(2,1)} fusion(bf16[256,384]{1,0:T(8,128)(2,1)} %collective-permute-done.14, bf16[4096,384]{1,0:T(8,128)(2,1)} %bitcast.186, bf16[256,384]{1,0:T(8,128)(2,1)S(1)} %collective-permute-done.13), kind=kLoop, calls=%fused_computation.18 | loop fusion | flops 10616832 | bytes 7077888 | tf_op jit(solution)/shard_map/concatenate | solution.py:39
  195.9 6.1 %gather_fusion.5 = bf16[64,128,384]{2,1,0:T(8,128)(2,1)} fusion(bf16[36,128,384]{2,1,0:T(8,128)(2,1)} %bitcast.178, s32[1024]{0:T(1024)S(1)} %pad_clamp_fusion), kind=kCustom, calls=%fused_computation.5 | custom fusion | bytes 12583168 | tf_op jit(solution)/shard_map/gather | solution.py:47
  201.9 5.0 %collective-permute-start.4 = (bf16[256,384]{1,0:T(8,128)(2,1)S(1)}, bf16[256,384]{1,0:T(8,128)(2,1)S(1)}, u32[]{:S(2)}, u32[]{:S(2)}) collective-permute-start(bf16[256,384]{1,0:T(8,128)(2,1)S(1)} %get-tuple-element.19), channel_id=1, source_target_pairs={{4,0},{8,4},{12,8},{16,12},{20,16},{24,20},{28,24},{32,28},{36,32}... | collective-permute-start | bytes 589832 | tf_op jit(solution)/shard_map/ppermute | solution.py:38
  207.0 5.0 %pad_maximum_fusion.3 = bf16[4608,384]{1,0:T(8,128)(2,1)} fusion(bf16[256,384]{1,0:T(8,128)(2,1)} %collective-permute-done.19, bf16[4096,384]{1,0:T(8,128)(2,1)} %bitcast.190, bf16[256,384]{1,0:T(8,128)(2,1)S(1)} %collective-permute-done.18), kind=kLoop, calls=%fused_computation.19 | loop fusion | flops 10616832 | bytes 7077888 | tf_op jit(solution)/shard_map/concatenate | solution.py:39
  212.0 6.1 %gather_fusion.7 = bf16[64,128,384]{2,1,0:T(8,128)(2,1)} fusion(bf16[36,128,384]{2,1,0:T(8,128)(2,1)} %bitcast.179, s32[1024]{0:T(1024)S(1)} %pad_clamp_fusion), kind=kCustom, calls=%fused_computation.7 | custom fusion | bytes 12583168 | tf_op jit(solution)/shard_map/gather | solution.py:47
  218.1 5.3 %bitcast_multiply_fusion.5 = f32[8,384,128]{1,2,0:T(8,128)} fusion(bf16[8,8,128,128]{3,2,1,0:T(8,128)(2,1)S(1)} %bitcast.161, bf16[8,8,128,384]{3,2,1,0:T(8,128)(2,1)} %bitcast.169), kind=kOutput, calls=%fused_computation.55 | convolution fusion | flops 805699584 | bytes 9961472 | tf_op jit(solution)/shard_map/rsij,rsjc->ric/dot_general | solution.py:48
  225.9 6.3 %pad_maximum_fusion.1 = bf16[4608,384]{1,0:T(8,128)(2,1)} fusion(bf16[256,384]{1,0:T(8,128)(2,1)S(1)} %collective-permute-done.9, bf16[4096,384]{1,0:T(8,128)(2,1)S(1)} %bitcast.194, bf16[256,384]{1,0:T(8,128)(2,1)S(1)} %collective-permute-done.8), kind=kLoop, calls=%fused_computation.17 | loop fusion | flops 10616832 | bytes 7077888 | tf_op jit(solution)/shard_map/concatenate | solution.py:39
  232.2 6.1 %gather_fusion.3 = bf16[64,128,384]{2,1,0:T(8,128)(2,1)} fusion(bf16[36,128,384]{2,1,0:T(8,128)(2,1)} %bitcast.180, s32[1024]{0:T(1024)S(1)} %pad_clamp_fusion), kind=kCustom, calls=%fused_computation.3 | custom fusion | bytes 12583168 | tf_op jit(solution)/shard_map/gather | solution.py:47
  238.3 5.3 %bitcast_multiply_fusion.6 = f32[8,384,128]{1,2,0:T(8,128)} fusion(bf16[8,8,128,128]{3,2,1,0:T(8,128)(2,1)S(1)} %bitcast.163, bf16[8,8,128,384]{3,2,1,0:T(8,128)(2,1)} %bitcast.172), kind=kOutput, calls=%fused_computation.56 | convolution fusion | flops 805699584 | bytes 9961472 | tf_op jit(solution)/shard_map/rsij,rsjc->ric/dot_general | solution.py:48
  243.6 6.5 %pad_maximum_fusion = bf16[4608,384]{1,0:T(8,128)(2,1)} fusion(bf16[256,384]{1,0:T(8,128)(2,1)S(1)} %collective-permute-done.4, bf16[4096,384]{1,0:T(8,128)(2,1)S(1)} %bitcast.200, bf16[256,384]{1,0:T(8,128)(2,1)S(1)} %collective-permute-done.3), kind=kLoop, calls=%fused_computation.16 | loop fusion | flops 10616832 | bytes 7077888 | tf_op jit(solution)/shard_map/concatenate | solution.py:39
  250.1 6.1 %gather_fusion.1 = bf16[64,128,384]{2,1,0:T(8,128)(2,1)} fusion(bf16[36,128,384]{2,1,0:T(8,128)(2,1)} %bitcast.181, s32[1024]{0:T(1024)S(1)} %pad_clamp_fusion), kind=kCustom, calls=%fused_computation.1 | custom fusion | bytes 12583168 | tf_op jit(solution)/shard_map/gather | solution.py:47
  256.2 4.2 bitcast_multiply_fusion.7
  263.3 3.2 collective-permute-start.37
  266.5 18.4 %collective-permute-done.35 = bf16[1024,384]{1,0:T(8,128)(2,1)S(1)} collective-permute-done((bf16[1024,384]{1,0:T(8,128)(2,1)S(1)}, bf16[1024,384]{1,0:T(8,128)(2,1)S(1)}, u32[]{:S(2)}, u32[]{:S(2)}) %collective-permute-start.35) | collective-permute-done | bytes 786464 | tf_op jit(solution)/shard_map/ppermute | solution.py:24
  284.9 3.2 collective-permute-start.32
  288.1 13.7 %collective-permute-done.30 = bf16[1024,384]{1,0:T(8,128)(2,1)} collective-permute-done((bf16[1024,384]{1,0:T(8,128)(2,1)}, bf16[1024,384]{1,0:T(8,128)(2,1)}, u32[]{:S(2)}, u32[]{:S(2)}) %collective-permute-start.30) | collective-permute-done | bytes 786464 | tf_op jit(solution)/shard_map/ppermute | solution.py:24
  301.8 2.9 pad_maximum_fusion.12
  304.7 13.9 %collective-permute-done.25 = bf16[1024,384]{1,0:T(8,128)(2,1)} collective-permute-done((bf16[1024,384]{1,0:T(8,128)(2,1)}, bf16[1024,384]{1,0:T(8,128)(2,1)}, u32[]{:S(2)}, u32[]{:S(2)}) %collective-permute-start.25) | collective-permute-done | bytes 786464 | tf_op jit(solution)/shard_map/ppermute | solution.py:24
  318.7 16.7 %collective-permute-done.36 = bf16[1024,384]{1,0:T(8,128)(2,1)S(1)} collective-permute-done((bf16[1024,384]{1,0:T(8,128)(2,1)S(1)}, bf16[1024,384]{1,0:T(8,128)(2,1)S(1)}, u32[]{:S(2)}, u32[]{:S(2)}) %collective-permute-start.36) | collective-permute-done | bytes 786464 | tf_op jit(solution)/shard_map/ppermute | solution.py:24
  337.3 4.5 gather_fusion.14
  343.7 3.2 collective-permute-start.22
  346.9 5.5 %collective-permute-done.20 = bf16[1024,384]{1,0:T(8,128)(2,1)} collective-permute-done((bf16[1024,384]{1,0:T(8,128)(2,1)S(1)}, bf16[1024,384]{1,0:T(8,128)(2,1)}, u32[]{:S(2)}, u32[]{:S(2)}) %collective-permute-start.20) | collective-permute-done | bytes 786464 | tf_op jit(solution)/shard_map/ppermute | solution.py:24
  352.4 16.8 %collective-permute-done.31 = bf16[1024,384]{1,0:T(8,128)(2,1)} collective-permute-done((bf16[1024,384]{1,0:T(8,128)(2,1)}, bf16[1024,384]{1,0:T(8,128)(2,1)}, u32[]{:S(2)}, u32[]{:S(2)}) %collective-permute-start.31) | collective-permute-done | bytes 786464 | tf_op jit(solution)/shard_map/ppermute | solution.py:24
  369.2 3.7 pad_maximum_fusion.15
  372.9 4.5 gather_fusion.12
  379.3 5.0 %collective-permute-start.39 = (bf16[256,384]{1,0:T(8,128)(2,1)}, bf16[256,384]{1,0:T(8,128)(2,1)}, u32[]{:S(2)}, u32[]{:S(2)}) collective-permute-start(bf16[256,384]{1,0:T(8,128)(2,1)} %get-tuple-element.13), channel_id=1, source_target_pairs={{4,0},{8,4},{12,8},{16,12},{20,16},{24,20},{28,24},{32,28},{36,32}... | collective-permute-start | bytes 589832 | tf_op jit(solution)/shard_map/ppermute | solution.py:38
  386.1 3.3 pad_maximum_fusion.14
  389.4 4.6 gather_fusion.10
  395.8 5.1 %collective-permute-start.34 = (bf16[256,384]{1,0:T(8,128)(2,1)}, bf16[256,384]{1,0:T(8,128)(2,1)}, u32[]{:S(2)}, u32[]{:S(2)}) collective-permute-start(bf16[256,384]{1,0:T(8,128)(2,1)} %get-tuple-element.11), channel_id=1, source_target_pairs={{4,0},{8,4},{12,8},{16,12},{20,16},{24,20},{28,24},{32,28},{36,32}... | collective-permute-start | bytes 589832 | tf_op jit(solution)/shard_map/ppermute | solution.py:38
  400.9 3.1 pad_maximum_fusion.13
  404.0 4.5 gather_fusion.8
  410.3 5.1 %collective-permute-start.29 = (bf16[256,384]{1,0:T(8,128)(2,1)S(1)}, bf16[256,384]{1,0:T(8,128)(2,1)S(1)}, u32[]{:S(2)}, u32[]{:S(2)}) collective-permute-start(bf16[256,384]{1,0:T(8,128)(2,1)S(1)} %copy-done.16), channel_id=1, source_target_pairs={{4,0},{8,4},{12,8},{16,12},{20,16},{24,20},{28,24},{32,28},{36,32}... | collective-permute-start | bytes 589832 | tf_op jit(solution)/shard_map/ppermute | solution.py:38
  415.4 5.0 %pad_maximum_fusion.7 = bf16[4608,384]{1,0:T(8,128)(2,1)} fusion(bf16[256,384]{1,0:T(8,128)(2,1)} %collective-permute-done.39, bf16[4096,384]{1,0:T(8,128)(2,1)} %bitcast.188, bf16[256,384]{1,0:T(8,128)(2,1)S(1)} %collective-permute-done.38), kind=kLoop, calls=%fused_computation.23 | loop fusion | flops 10616832 | bytes 7077888 | tf_op jit(solution)/shard_map/concatenate | solution.py:39
  420.4 6.1 %gather_fusion.15 = bf16[64,128,384]{2,1,0:T(8,128)(2,1)} fusion(bf16[36,128,384]{2,1,0:T(8,128)(2,1)} %bitcast.182, s32[1024]{0:T(1024)S(1)} %pad_clamp_fusion), kind=kCustom, calls=%fused_computation.15 | custom fusion | bytes 12583168 | tf_op jit(solution)/shard_map/gather | solution.py:47
  426.4 5.4 %bitcast_multiply_fusion = f32[8,384,128]{1,2,0:T(8,128)} fusion(bf16[8,8,128,128]{3,2,1,0:T(8,128)(2,1)S(1)} %bitcast.165, bf16[8,8,128,384]{3,2,1,0:T(8,128)(2,1)} %bitcast.174), kind=kOutput, calls=%fused_computation.50 | convolution fusion | flops 805699584 | bytes 9961472 | tf_op jit(solution)/shard_map/rsij,rsjc->ric/dot_general | solution.py:48
  431.8 5.0 %collective-permute-start.24 = (bf16[256,384]{1,0:T(8,128)(2,1)S(1)}, bf16[256,384]{1,0:T(8,128)(2,1)S(1)}, u32[]{:S(2)}, u32[]{:S(2)}) collective-permute-start(bf16[256,384]{1,0:T(8,128)(2,1)S(1)} %get-tuple-element.7), channel_id=1, source_target_pairs={{4,0},{8,4},{12,8},{16,12},{20,16},{24,20},{28,24},{32,28},{36,32}... | collective-permute-start | bytes 589832 | tf_op jit(solution)/shard_map/ppermute | solution.py:38
  436.9 4.3 pad_maximum_fusion.6
  441.2 6.1 %gather_fusion.13 = bf16[64,128,384]{2,1,0:T(8,128)(2,1)} fusion(bf16[36,128,384]{2,1,0:T(8,128)(2,1)} %bitcast.183, s32[1024]{0:T(1024)S(1)} %pad_clamp_fusion), kind=kCustom, calls=%fused_computation.13 | custom fusion | bytes 12583168 | tf_op jit(solution)/shard_map/gather | solution.py:47
  447.3 5.3 %bitcast_multiply_fusion.1 = f32[8,384,128]{1,2,0:T(8,128)} fusion(bf16[8,8,128,128]{3,2,1,0:T(8,128)(2,1)S(1)} %bitcast.166, bf16[8,8,128,384]{3,2,1,0:T(8,128)(2,1)} %bitcast.175), kind=kOutput, calls=%fused_computation.51 | convolution fusion | flops 805699584 | bytes 9961472 | tf_op jit(solution)/shard_map/rsij,rsjc->ric/dot_general | solution.py:48
  452.6 6.3 %pad_maximum_fusion.5 = bf16[4608,384]{1,0:T(8,128)(2,1)} fusion(bf16[256,384]{1,0:T(8,128)(2,1)S(1)} %collective-permute-done.29, bf16[4096,384]{1,0:T(8,128)(2,1)S(1)} %bitcast.196, bf16[256,384]{1,0:T(8,128)(2,1)S(1)} %collective-permute-done.28), kind=kLoop, calls=%fused_computation.21 | loop fusion | flops 10616832 | bytes 7077888 | tf_op jit(solution)/shard_map/concatenate | solution.py:39
  458.9 6.1 %gather_fusion.11 = bf16[64,128,384]{2,1,0:T(8,128)(2,1)} fusion(bf16[36,128,384]{2,1,0:T(8,128)(2,1)} %bitcast.184, s32[1024]{0:T(1024)S(1)} %pad_clamp_fusion), kind=kCustom, calls=%fused_computation.11 | custom fusion | bytes 12583168 | tf_op jit(solution)/shard_map/gather | solution.py:47
  465.0 5.3 %bitcast_multiply_fusion.2 = f32[8,384,128]{1,2,0:T(8,128)} fusion(bf16[8,8,128,128]{3,2,1,0:T(8,128)(2,1)S(1)} %bitcast.167, bf16[8,8,128,384]{3,2,1,0:T(8,128)(2,1)} %bitcast.176), kind=kOutput, calls=%fused_computation.52 | convolution fusion | flops 805699584 | bytes 9961472 | tf_op jit(solution)/shard_map/rsij,rsjc->ric/dot_general | solution.py:48
  470.3 6.5 %pad_maximum_fusion.4 = bf16[4608,384]{1,0:T(8,128)(2,1)} fusion(bf16[256,384]{1,0:T(8,128)(2,1)S(1)} %collective-permute-done.24, bf16[4096,384]{1,0:T(8,128)(2,1)S(1)} %bitcast.198, bf16[256,384]{1,0:T(8,128)(2,1)S(1)} %collective-permute-done.23), kind=kLoop, calls=%fused_computation.20 | loop fusion | flops 10616832 | bytes 7077888 | tf_op jit(solution)/shard_map/concatenate | solution.py:39
  476.8 6.1 %gather_fusion.9 = bf16[64,128,384]{2,1,0:T(8,128)(2,1)} fusion(bf16[36,128,384]{2,1,0:T(8,128)(2,1)} %bitcast.177, s32[1024]{0:T(1024)S(1)} %pad_clamp_fusion), kind=kCustom, calls=%fused_computation.9 | custom fusion | bytes 12583168 | tf_op jit(solution)/shard_map/gather | solution.py:47
  482.9 4.2 bitcast_multiply_fusion.3
  (118 shorter events, 39.4 us)
Async XLA Ops:
  0.6 27.3 %copy-start.17 = (s32[32,2]{0,1:T(2,128)S(1)}, s32[32,2]{0,1:T(2,128)}, u32[]{:S(2)}) copy-start(s32[32,2]{0,1:T(2,128)} %param.5) | copy-start | bytes 772
  5.1 22.9 %collective-permute-start.10 = (bf16[1024,384]{1,0:T(8,128)(2,1)}, bf16[1024,384]{1,0:T(8,128)(2,1)}, u32[]{:S(2)}, u32[]{:S(2)}) collective-permute-start(bf16[1024,384]{1,0:T(8,128)(2,1)} %get-tuple-element.27), channel_id=1, source_target_pairs={{0,1},{1,2},{2,3},{3,0},{4,5},{5,6},{6,7},{7,4},{8,9},{9,10},{10,1... | collective-permute-start | bytes 2359304 | tf_op jit(solution)/shard_map/ppermute | solution.py:24
  7.1 78.5 %collective-permute-start.12 = (bf16[1024,384]{1,0:T(8,128)(2,1)}, bf16[1024,384]{1,0:T(8,128)(2,1)}, u32[]{:S(2)}, u32[]{:S(2)}) collective-permute-start(bf16[1024,384]{1,0:T(8,128)(2,1)} %get-tuple-element.27), channel_id=1, source_target_pairs={{1,0},{2,1},{3,2},{0,3},{5,4},{6,5},{7,6},{4,7},{9,8},{10,9},{11,1... | collective-permute-start | bytes 2359304 | tf_op jit(solution)/shard_map/ppermute | solution.py:26
  9.3 76.4 %collective-permute-start.15 = (bf16[1024,384]{1,0:T(8,128)(2,1)}, bf16[1024,384]{1,0:T(8,128)(2,1)}, u32[]{:S(2)}, u32[]{:S(2)}) collective-permute-start(bf16[1024,384]{1,0:T(8,128)(2,1)} %get-tuple-element.26), channel_id=1, source_target_pairs={{0,1},{1,2},{2,3},{3,0},{4,5},{5,6},{6,7},{7,4},{8,9},{9,10},{10,1... | collective-permute-start | bytes 2359304 | tf_op jit(solution)/shard_map/ppermute | solution.py:24
  9.3 77.4 %collective-permute-start.5 = (bf16[1024,384]{1,0:T(8,128)(2,1)}, bf16[1024,384]{1,0:T(8,128)(2,1)}, u32[]{:S(2)}, u32[]{:S(2)}) collective-permute-start(bf16[1024,384]{1,0:T(8,128)(2,1)} %get-tuple-element.24), channel_id=1, source_target_pairs={{0,1},{1,2},{2,3},{3,0},{4,5},{5,6},{6,7},{7,4},{8,9},{9,10},{10,1... | collective-permute-start | bytes 2359304 | tf_op jit(solution)/shard_map/ppermute | solution.py:24
  27.9 61.3 %collective-permute-start.11 = (bf16[1024,384]{1,0:T(8,128)(2,1)}, bf16[1024,384]{1,0:T(8,128)(2,1)}, u32[]{:S(2)}, u32[]{:S(2)}) collective-permute-start(bf16[1024,384]{1,0:T(8,128)(2,1)} %collective-permute-done.10), channel_id=1, source_target_pairs={{0,1},{1,2},{2,3},{3,0},{4,5},{5,6},{6,7},{7,4},{8,9},{9,10},{10,1... | collective-permute-start | bytes 2359304 | tf_op jit(solution)/shard_map/ppermute | solution.py:24
  78.8 68.1 %all-to-all-start.1 = ((bf16[32,2,128,128]{3,2,1,0:T(8,128)(2,1)}), bf16[32,2,128,128]{3,2,1,0:T(8,128)(2,1)S(1)}, u32[]{:S(2)}, u32[]{:S(2)}) async-start(bf16[32,2,128,128]{3,2,1,0:T(8,128)(2,1)} %param.4), calls=%async_computation.1 | async-start | bytes 4194304 | tf_op jit(solution)/shard_map/all_to_all | solution.py:57
  82.4 43.2 %collective-permute-start.17 = (bf16[1024,384]{1,0:T(8,128)(2,1)}, bf16[1024,384]{1,0:T(8,128)(2,1)}, u32[]{:S(2)}, u32[]{:S(2)}) collective-permute-start(bf16[1024,384]{1,0:T(8,128)(2,1)} %get-tuple-element.26), channel_id=1, source_target_pairs={{1,0},{2,1},{3,2},{0,3},{5,4},{6,5},{7,6},{4,7},{9,8},{10,9},{11,1... | collective-permute-start | bytes 2359304 | tf_op jit(solution)/shard_map/ppermute | solution.py:26
  85.6 41.2 %collective-permute-start = (bf16[1024,384]{1,0:T(8,128)(2,1)}, bf16[1024,384]{1,0:T(8,128)(2,1)}, u32[]{:S(2)}, u32[]{:S(2)}) collective-permute-start(bf16[1024,384]{1,0:T(8,128)(2,1)} %get-tuple-element.25), channel_id=1, source_target_pairs={{0,1},{1,2},{2,3},{3,0},{4,5},{5,6},{6,7},{7,4},{8,9},{9,10},{10,1... | collective-permute-start | bytes 2359304 | tf_op jit(solution)/shard_map/ppermute | solution.py:24
  85.7 57.9 %collective-permute-start.16 = (bf16[1024,384]{1,0:T(8,128)(2,1)}, bf16[1024,384]{1,0:T(8,128)(2,1)}, u32[]{:S(2)}, u32[]{:S(2)}) collective-permute-start(bf16[1024,384]{1,0:T(8,128)(2,1)} %collective-permute-done.15), channel_id=1, source_target_pairs={{0,1},{1,2},{2,3},{3,0},{4,5},{5,6},{6,7},{7,4},{8,9},{9,10},{10,1... | collective-permute-start | bytes 2359304 | tf_op jit(solution)/shard_map/ppermute | solution.py:24
  86.7 69.7 %collective-permute-start.7 = (bf16[1024,384]{1,0:T(8,128)(2,1)}, bf16[1024,384]{1,0:T(8,128)(2,1)}, u32[]{:S(2)}, u32[]{:S(2)}) collective-permute-start(bf16[1024,384]{1,0:T(8,128)(2,1)} %get-tuple-element.24), channel_id=1, source_target_pairs={{1,0},{2,1},{3,2},{0,3},{5,4},{6,5},{7,6},{4,7},{9,8},{10,9},{11,1... | collective-permute-start | bytes 2359304 | tf_op jit(solution)/shard_map/ppermute | solution.py:26
  89.3 72.2 %collective-permute-start.6 = (bf16[1024,384]{1,0:T(8,128)(2,1)}, bf16[1024,384]{1,0:T(8,128)(2,1)}, u32[]{:S(2)}, u32[]{:S(2)}) collective-permute-start(bf16[1024,384]{1,0:T(8,128)(2,1)} %collective-permute-done.5), channel_id=1, source_target_pairs={{0,1},{1,2},{2,3},{3,0},{4,5},{5,6},{6,7},{7,4},{8,9},{9,10},{10,1... | collective-permute-start | bytes 2359304 | tf_op jit(solution)/shard_map/ppermute | solution.py:24
  125.6 45.5 %collective-permute-start.2 = (bf16[1024,384]{1,0:T(8,128)(2,1)}, bf16[1024,384]{1,0:T(8,128)(2,1)}, u32[]{:S(2)}, u32[]{:S(2)}) collective-permute-start(bf16[1024,384]{1,0:T(8,128)(2,1)} %get-tuple-element.25), channel_id=1, source_target_pairs={{1,0},{2,1},{3,2},{0,3},{5,4},{6,5},{7,6},{4,7},{9,8},{10,9},{11,1... | collective-permute-start | bytes 2359304 | tf_op jit(solution)/shard_map/ppermute | solution.py:26
  126.8 49.4 %collective-permute-start.1 = (bf16[1024,384]{1,0:T(8,128)(2,1)}, bf16[1024,384]{1,0:T(8,128)(2,1)}, u32[]{:S(2)}, u32[]{:S(2)}) collective-permute-start(bf16[1024,384]{1,0:T(8,128)(2,1)} %collective-permute-done), channel_id=1, source_target_pairs={{0,1},{1,2},{2,3},{3,0},{4,5},{5,6},{6,7},{7,4},{8,9},{9,10},{10,1... | collective-permute-start | bytes 2359304 | tf_op jit(solution)/shard_map/ppermute | solution.py:24
  143.6 42.0 %collective-permute-start.13 = (bf16[256,384]{1,0:T(8,128)(2,1)}, bf16[256,384]{1,0:T(8,128)(2,1)S(1)}, u32[]{:S(2)}, u32[]{:S(2)}) collective-permute-start(bf16[256,384]{1,0:T(8,128)(2,1)} %get-tuple-element.30), channel_id=1, source_target_pairs={{0,4},{4,8},{8,12},{12,16},{16,20},{20,24},{24,28},{28,32},{32,36}... | collective-permute-start | bytes 589832 | tf_op jit(solution)/shard_map/ppermute | solution.py:37
  146.9 1.3 copy-start.7
  156.4 34.3 %collective-permute-start.14 = (bf16[256,384]{1,0:T(8,128)(2,1)}, bf16[256,384]{1,0:T(8,128)(2,1)}, u32[]{:S(2)}, u32[]{:S(2)}) collective-permute-start(bf16[256,384]{1,0:T(8,128)(2,1)} %get-tuple-element.31), channel_id=1, source_target_pairs={{4,0},{8,4},{12,8},{16,12},{20,16},{24,20},{28,24},{32,28},{36,32}... | collective-permute-start | bytes 589832 | tf_op jit(solution)/shard_map/ppermute | solution.py:38
  161.5 40.4 %collective-permute-start.18 = (bf16[256,384]{1,0:T(8,128)(2,1)}, bf16[256,384]{1,0:T(8,128)(2,1)S(1)}, u32[]{:S(2)}, u32[]{:S(2)}) collective-permute-start(bf16[256,384]{1,0:T(8,128)(2,1)} %get-tuple-element.32), channel_id=1, source_target_pairs={{0,4},{4,8},{8,12},{12,16},{16,20},{20,24},{24,28},{28,32},{32,36}... | collective-permute-start | bytes 589832 | tf_op jit(solution)/shard_map/ppermute | solution.py:37
  171.1 35.9 %collective-permute-start.19 = (bf16[256,384]{1,0:T(8,128)(2,1)}, bf16[256,384]{1,0:T(8,128)(2,1)}, u32[]{:S(2)}, u32[]{:S(2)}) collective-permute-start(bf16[256,384]{1,0:T(8,128)(2,1)} %get-tuple-element.33), channel_id=1, source_target_pairs={{4,0},{8,4},{12,8},{16,12},{20,16},{24,20},{28,24},{32,28},{36,32}... | collective-permute-start | bytes 589832 | tf_op jit(solution)/shard_map/ppermute | solution.py:38
  176.1 49.8 %collective-permute-start.8 = (bf16[256,384]{1,0:T(8,128)(2,1)}, bf16[256,384]{1,0:T(8,128)(2,1)S(1)}, u32[]{:S(2)}, u32[]{:S(2)}) collective-permute-start(bf16[256,384]{1,0:T(8,128)(2,1)} %get-tuple-element.28), channel_id=1, source_target_pairs={{0,4},{4,8},{8,12},{12,16},{16,20},{20,24},{24,28},{28,32},{32,36}... | collective-permute-start | bytes 589832 | tf_op jit(solution)/shard_map/ppermute | solution.py:37
  179.3 6.3 %copy-start.15 = (bf16[256,384]{1,0:T(8,128)(2,1)S(1)}, bf16[256,384]{1,0:T(8,128)(2,1)}, u32[]{:S(2)}) copy-start(bf16[256,384]{1,0:T(8,128)(2,1)} %get-tuple-element.29) | copy-start | bytes 589828
  185.6 40.3 %collective-permute-start.9 = (bf16[256,384]{1,0:T(8,128)(2,1)S(1)}, bf16[256,384]{1,0:T(8,128)(2,1)S(1)}, u32[]{:S(2)}, u32[]{:S(2)}) collective-permute-start(bf16[256,384]{1,0:T(8,128)(2,1)S(1)} %copy-done.15), channel_id=1, source_target_pairs={{4,0},{8,4},{12,8},{16,12},{20,16},{24,20},{28,24},{32,28},{36,32}... | collective-permute-start | bytes 589832 | tf_op jit(solution)/shard_map/ppermute | solution.py:38
  190.7 52.9 %collective-permute-start.3 = (bf16[256,384]{1,0:T(8,128)(2,1)}, bf16[256,384]{1,0:T(8,128)(2,1)S(1)}, u32[]{:S(2)}, u32[]{:S(2)}) collective-permute-start(bf16[256,384]{1,0:T(8,128)(2,1)} %get-tuple-element.18), channel_id=1, source_target_pairs={{0,4},{4,8},{8,12},{12,16},{16,20},{20,24},{24,28},{28,32},{32,36}... | collective-permute-start | bytes 589832 | tf_op jit(solution)/shard_map/ppermute | solution.py:37
  201.9 41.7 %collective-permute-start.4 = (bf16[256,384]{1,0:T(8,128)(2,1)S(1)}, bf16[256,384]{1,0:T(8,128)(2,1)S(1)}, u32[]{:S(2)}, u32[]{:S(2)}) collective-permute-start(bf16[256,384]{1,0:T(8,128)(2,1)S(1)} %get-tuple-element.19), channel_id=1, source_target_pairs={{4,0},{8,4},{12,8},{16,12},{20,16},{24,20},{28,24},{32,28},{36,32}... | collective-permute-start | bytes 589832 | tf_op jit(solution)/shard_map/ppermute | solution.py:38
  218.1 5.4 %copy-start = (bf16[64,128,384]{2,1,0:T(8,128)(2,1)S(1)}, bf16[64,128,384]{2,1,0:T(8,128)(2,1)}, u32[]{:S(2)}) copy-start(bf16[64,128,384]{2,1,0:T(8,128)(2,1)} %gather_fusion.7) | copy-start | bytes 18874372
  223.4 2.5 copy-start.2
  238.3 5.4 %copy-start.5 = (bf16[4,1024,384]{2,1,0:T(8,128)(2,1)S(1)}, bf16[4,1024,384]{2,1,0:T(8,128)(2,1)}, u32[]{:S(2)}) copy-start(bf16[4,1024,384]{2,1,0:T(8,128)(2,1)} %gather_fusion) | copy-start | bytes 9437188
  256.2 4.2 copy-start.10
  256.2 4.2 copy-start.11
  256.2 4.2 copy-start.13
  256.2 5.1 %copy-start.14 = (bf16[1024,1536]{1,0:T(8,128)(2,1)S(1)}, bf16[1024,1536]{1,0:T(8,128)(2,1)}, u32[]{:S(2)}) copy-start(bf16[1024,1536]{1,0:T(8,128)(2,1)} %param.7) | copy-start | bytes 9437188
  263.3 21.6 %collective-permute-start.35 = (bf16[1024,384]{1,0:T(8,128)(2,1)S(1)}, bf16[1024,384]{1,0:T(8,128)(2,1)S(1)}, u32[]{:S(2)}, u32[]{:S(2)}) collective-permute-start(bf16[1024,384]{1,0:T(8,128)(2,1)S(1)} %get-tuple-element.16), channel_id=1, source_target_pairs={{0,1},{1,2},{2,3},{3,0},{4,5},{5,6},{6,7},{7,4},{8,9},{9,10},{10,1... | collective-permute-start | bytes 2359304 | tf_op jit(solution)/shard_map/ppermute | solution.py:24
  263.3 24.9 %collective-permute-start.37 = (bf16[1024,384]{1,0:T(8,128)(2,1)S(1)}, bf16[1024,384]{1,0:T(8,128)(2,1)S(1)}, u32[]{:S(2)}, u32[]{:S(2)}) collective-permute-start(bf16[1024,384]{1,0:T(8,128)(2,1)S(1)} %get-tuple-element.16), channel_id=1, source_target_pairs={{1,0},{2,1},{3,2},{0,3},{5,4},{6,5},{7,6},{4,7},{9,8},{10,9},{11,1... | collective-permute-start | bytes 2359304 | tf_op jit(solution)/shard_map/ppermute | solution.py:26
  266.5 35.3 %collective-permute-start.30 = (bf16[1024,384]{1,0:T(8,128)(2,1)}, bf16[1024,384]{1,0:T(8,128)(2,1)}, u32[]{:S(2)}, u32[]{:S(2)}) collective-permute-start(bf16[1024,384]{1,0:T(8,128)(2,1)} %get-tuple-element.17), channel_id=1, source_target_pairs={{0,1},{1,2},{2,3},{3,0},{4,5},{5,6},{6,7},{7,4},{8,9},{9,10},{10,1... | collective-permute-start | bytes 2359304 | tf_op jit(solution)/shard_map/ppermute | solution.py:24
  266.5 52.2 %collective-permute-start.25 = (bf16[1024,384]{1,0:T(8,128)(2,1)}, bf16[1024,384]{1,0:T(8,128)(2,1)}, u32[]{:S(2)}, u32[]{:S(2)}) collective-permute-start(bf16[1024,384]{1,0:T(8,128)(2,1)} %get-tuple-element.15), channel_id=1, source_target_pairs={{0,1},{1,2},{2,3},{3,0},{4,5},{5,6},{6,7},{7,4},{8,9},{9,10},{10,1... | collective-permute-start | bytes 2359304 | tf_op jit(solution)/shard_map/ppermute | solution.py:24
  284.9 50.6 %collective-permute-start.36 = (bf16[1024,384]{1,0:T(8,128)(2,1)S(1)}, bf16[1024,384]{1,0:T(8,128)(2,1)S(1)}, u32[]{:S(2)}, u32[]{:S(2)}) collective-permute-start(bf16[1024,384]{1,0:T(8,128)(2,1)S(1)} %collective-permute-done.35), channel_id=1, source_target_pairs={{0,1},{1,2},{2,3},{3,0},{4,5},{5,6},{6,7},{7,4},{8,9},{9,10},{10,1... | collective-permute-start | bytes 2359304 | tf_op jit(solution)/shard_map/ppermute | solution.py:24
  284.9 58.8 %collective-permute-start.32 = (bf16[1024,384]{1,0:T(8,128)(2,1)}, bf16[1024,384]{1,0:T(8,128)(2,1)}, u32[]{:S(2)}, u32[]{:S(2)}) collective-permute-start(bf16[1024,384]{1,0:T(8,128)(2,1)} %get-tuple-element.17), channel_id=1, source_target_pairs={{1,0},{2,1},{3,2},{0,3},{5,4},{6,5},{7,6},{4,7},{9,8},{10,9},{11,1... | collective-permute-start | bytes 2359304 | tf_op jit(solution)/shard_map/ppermute | solution.py:26
  288.1 64.3 %collective-permute-start.20 = (bf16[1024,384]{1,0:T(8,128)(2,1)S(1)}, bf16[1024,384]{1,0:T(8,128)(2,1)}, u32[]{:S(2)}, u32[]{:S(2)}) collective-permute-start(bf16[1024,384]{1,0:T(8,128)(2,1)S(1)} %get-tuple-element.14), channel_id=1, source_target_pairs={{0,1},{1,2},{2,3},{3,0},{4,5},{5,6},{6,7},{7,4},{8,9},{9,10},{10,1... | collective-permute-start | bytes 2359304 | tf_op jit(solution)/shard_map/ppermute | solution.py:24
  301.8 67.4 %collective-permute-start.31 = (bf16[1024,384]{1,0:T(8,128)(2,1)}, bf16[1024,384]{1,0:T(8,128)(2,1)}, u32[]{:S(2)}, u32[]{:S(2)}) collective-permute-start(bf16[1024,384]{1,0:T(8,128)(2,1)} %collective-permute-done.30), channel_id=1, source_target_pairs={{0,1},{1,2},{2,3},{3,0},{4,5},{5,6},{6,7},{7,4},{8,9},{9,10},{10,1... | collective-permute-start | bytes 2359304 | tf_op jit(solution)/shard_map/ppermute | solution.py:24
  318.7 60.6 %collective-permute-start.27 = (bf16[1024,384]{1,0:T(8,128)(2,1)}, bf16[1024,384]{1,0:T(8,128)(2,1)}, u32[]{:S(2)}, u32[]{:S(2)}) collective-permute-start(bf16[1024,384]{1,0:T(8,128)(2,1)} %get-tuple-element.15), channel_id=1, source_target_pairs={{1,0},{2,1},{3,2},{0,3},{5,4},{6,5},{7,6},{4,7},{9,8},{10,9},{11,1... | collective-permute-start | bytes 2359304 | tf_op jit(solution)/shard_map/ppermute | solution.py:26
  335.4 50.7 %collective-permute-start.26 = (bf16[1024,384]{1,0:T(8,128)(2,1)}, bf16[1024,384]{1,0:T(8,128)(2,1)}, u32[]{:S(2)}, u32[]{:S(2)}) collective-permute-start(bf16[1024,384]{1,0:T(8,128)(2,1)} %collective-permute-done.25), channel_id=1, source_target_pairs={{0,1},{1,2},{2,3},{3,0},{4,5},{5,6},{6,7},{7,4},{8,9},{9,10},{10,1... | collective-permute-start | bytes 2359304 | tf_op jit(solution)/shard_map/ppermute | solution.py:24
  343.7 52.1 %collective-permute-start.22 = (bf16[1024,384]{1,0:T(8,128)(2,1)S(1)}, bf16[1024,384]{1,0:T(8,128)(2,1)}, u32[]{:S(2)}, u32[]{:S(2)}) collective-permute-start(bf16[1024,384]{1,0:T(8,128)(2,1)S(1)} %get-tuple-element.14), channel_id=1, source_target_pairs={{1,0},{2,1},{3,2},{0,3},{5,4},{6,5},{7,6},{4,7},{9,8},{10,9},{11,1... | collective-permute-start | bytes 2359304 | tf_op jit(solution)/shard_map/ppermute | solution.py:26
  352.4 48.5 %collective-permute-start.21 = (bf16[1024,384]{1,0:T(8,128)(2,1)}, bf16[1024,384]{1,0:T(8,128)(2,1)}, u32[]{:S(2)}, u32[]{:S(2)}) collective-permute-start(bf16[1024,384]{1,0:T(8,128)(2,1)} %collective-permute-done.20), channel_id=1, source_target_pairs={{0,1},{1,2},{2,3},{3,0},{4,5},{5,6},{6,7},{7,4},{8,9},{9,10},{10,1... | collective-permute-start | bytes 2359304 | tf_op jit(solution)/shard_map/ppermute | solution.py:24
  369.2 41.1 %collective-permute-start.38 = (bf16[256,384]{1,0:T(8,128)(2,1)}, bf16[256,384]{1,0:T(8,128)(2,1)S(1)}, u32[]{:S(2)}, u32[]{:S(2)}) collective-permute-start(bf16[256,384]{1,0:T(8,128)(2,1)} %get-tuple-element.12), channel_id=1, source_target_pairs={{0,4},{4,8},{8,12},{12,16},{16,20},{20,24},{24,28},{28,32},{32,36}... | collective-permute-start | bytes 589832 | tf_op jit(solution)/shard_map/ppermute | solution.py:37
  379.3 36.1 %collective-permute-start.39 = (bf16[256,384]{1,0:T(8,128)(2,1)}, bf16[256,384]{1,0:T(8,128)(2,1)}, u32[]{:S(2)}, u32[]{:S(2)}) collective-permute-start(bf16[256,384]{1,0:T(8,128)(2,1)} %get-tuple-element.13), channel_id=1, source_target_pairs={{4,0},{8,4},{12,8},{16,12},{20,16},{24,20},{28,24},{32,28},{36,32}... | collective-permute-start | bytes 589832 | tf_op jit(solution)/shard_map/ppermute | solution.py:38
  386.1 45.7 %collective-permute-start.33 = (bf16[256,384]{1,0:T(8,128)(2,1)}, bf16[256,384]{1,0:T(8,128)(2,1)S(1)}, u32[]{:S(2)}, u32[]{:S(2)}) collective-permute-start(bf16[256,384]{1,0:T(8,128)(2,1)} %get-tuple-element.10), channel_id=1, source_target_pairs={{0,4},{4,8},{8,12},{12,16},{16,20},{20,24},{24,28},{28,32},{32,36}... | collective-permute-start | bytes 589832 | tf_op jit(solution)/shard_map/ppermute | solution.py:37
  395.8 41.1 %collective-permute-start.34 = (bf16[256,384]{1,0:T(8,128)(2,1)}, bf16[256,384]{1,0:T(8,128)(2,1)}, u32[]{:S(2)}, u32[]{:S(2)}) collective-permute-start(bf16[256,384]{1,0:T(8,128)(2,1)} %get-tuple-element.11), channel_id=1, source_target_pairs={{4,0},{8,4},{12,8},{16,12},{20,16},{24,20},{28,24},{32,28},{36,32}... | collective-permute-start | bytes 589832 | tf_op jit(solution)/shard_map/ppermute | solution.py:38
  400.9 51.7 %collective-permute-start.28 = (bf16[256,384]{1,0:T(8,128)(2,1)}, bf16[256,384]{1,0:T(8,128)(2,1)S(1)}, u32[]{:S(2)}, u32[]{:S(2)}) collective-permute-start(bf16[256,384]{1,0:T(8,128)(2,1)} %get-tuple-element.8), channel_id=1, source_target_pairs={{0,4},{4,8},{8,12},{12,16},{16,20},{20,24},{24,28},{28,32},{32,36}... | collective-permute-start | bytes 589832 | tf_op jit(solution)/shard_map/ppermute | solution.py:37
  404.0 6.3 %copy-start.16 = (bf16[256,384]{1,0:T(8,128)(2,1)S(1)}, bf16[256,384]{1,0:T(8,128)(2,1)}, u32[]{:S(2)}) copy-start(bf16[256,384]{1,0:T(8,128)(2,1)} %get-tuple-element.9) | copy-start | bytes 589828
  410.3 42.3 %collective-permute-start.29 = (bf16[256,384]{1,0:T(8,128)(2,1)S(1)}, bf16[256,384]{1,0:T(8,128)(2,1)S(1)}, u32[]{:S(2)}, u32[]{:S(2)}) collective-permute-start(bf16[256,384]{1,0:T(8,128)(2,1)S(1)} %copy-done.16), channel_id=1, source_target_pairs={{4,0},{8,4},{12,8},{16,12},{20,16},{24,20},{28,24},{32,28},{36,32}... | collective-permute-start | bytes 589832 | tf_op jit(solution)/shard_map/ppermute | solution.py:38
  415.4 55.0 %collective-permute-start.23 = (bf16[256,384]{1,0:T(8,128)(2,1)}, bf16[256,384]{1,0:T(8,128)(2,1)S(1)}, u32[]{:S(2)}, u32[]{:S(2)}) collective-permute-start(bf16[256,384]{1,0:T(8,128)(2,1)} %get-tuple-element.6), channel_id=1, source_target_pairs={{0,4},{4,8},{8,12},{12,16},{16,20},{20,24},{24,28},{28,32},{32,36}... | collective-permute-start | bytes 589832 | tf_op jit(solution)/shard_map/ppermute | solution.py:37
  426.4 10.4 %copy-start.1 = (bf16[4,1024,384]{2,1,0:T(8,128)(2,1)S(1)}, bf16[4,1024,384]{2,1,0:T(8,128)(2,1)}, u32[]{:S(2)}) copy-start(bf16[4,1024,384]{2,1,0:T(8,128)(2,1)} %gather_fusion.12) | copy-start | bytes 9437188
  431.8 38.5 %collective-permute-start.24 = (bf16[256,384]{1,0:T(8,128)(2,1)S(1)}, bf16[256,384]{1,0:T(8,128)(2,1)S(1)}, u32[]{:S(2)}, u32[]{:S(2)}) collective-permute-start(bf16[256,384]{1,0:T(8,128)(2,1)S(1)} %get-tuple-element.7), channel_id=1, source_target_pairs={{4,0},{8,4},{12,8},{16,12},{20,16},{24,20},{28,24},{32,28},{36,32}... | collective-permute-start | bytes 589832 | tf_op jit(solution)/shard_map/ppermute | solution.py:38
  447.3 5.4 %copy-start.3 = (bf16[4,1024,384]{2,1,0:T(8,128)(2,1)S(1)}, bf16[4,1024,384]{2,1,0:T(8,128)(2,1)}, u32[]{:S(2)}) copy-start(bf16[4,1024,384]{2,1,0:T(8,128)(2,1)} %gather_fusion.10) | copy-start | bytes 9437188
  465.0 5.4 %copy-start.4 = (bf16[4,1024,384]{2,1,0:T(8,128)(2,1)S(1)}, bf16[4,1024,384]{2,1,0:T(8,128)(2,1)}, u32[]{:S(2)}) copy-start(bf16[4,1024,384]{2,1,0:T(8,128)(2,1)} %gather_fusion.8) | copy-start | bytes 9437188
  482.9 4.2 copy-start.6
  482.9 4.2 copy-start.8
  482.9 4.6 copy-start.9
  482.9 5.1 %copy-start.12 = (f32[8,384,128]{1,2,0:T(8,128)S(1)}, f32[8,384,128]{1,2,0:T(8,128)}, u32[]{:S(2)}) copy-start(f32[8,384,128]{1,2,0:T(8,128)} %bitcast_multiply_fusion.2) | copy-start | bytes 4718596
